TPU v7x, 32 devices: a whole 2x2x4 slice. The times are simulated.
32 devices in a mesh: tile: 8 (over z, y), win: 4 (over x, core).
Axes of the slice: x: 2, y: 2, z: 4, core: 2. Of those that a mesh axis runs over, the one named last changes fastest.
Arguments:
- records: bfloat16 [16, 2048, 2048], P('win', 'tile'), may hold values from -6 to 6
- pair_first: int32 [2048], P('tile'), may hold values from 0 to 255
- pair_offset: int32 [2048], P('tile'), may hold values from 1 to 255
- owners: int32 [2048, 1], P('tile'), may hold values from 0 to 7; in each aligned block of 256 rows (0 to 255, 256 to 511, ...) at most 80 rows name the same one
Outputs:
- gathers: bfloat16 [8, 8, 80, 2048], P('tile', None, None, 'win')
Inputs may be any that keep to these rules, and one draw needn't show every extreme that they name: `owners`: among the 256 pairs of one tile no owner is named more than 80 times, and in every draw some tile names some owner exactly 80 times.
All inputs are finite; a program needn't handle non-finite values.
Results may differ from a plain program's by a relative error of at most 0.0066.
Values may be sent and summed in bfloat16 or wider, within the bound.
No kernel may reach another device: no remote copies, remote signals or barrier semaphores. Data moves between devices by JAX's collectives and lax.ppermute only.
A program may use at most 128 MiB of HBM per device.

v0:
```python
import math
import jax
import jax.numpy as jnp
from jax import lax
from jax.sharding import PartitionSpec as P

BAND = 64
power_floor = 1e-06


def phase_table(rows, col_count, length):
    split = 64 if col_count % 64 == 0 else 1
    coarse = jnp.arange(col_count // split, dtype=jnp.int32) * split
    fine = jnp.arange(split, dtype=jnp.int32)
    scale = 2.0 * math.pi / length
    coarse_angle = (rows[:, None] * coarse[None, :] % length).astype(jnp.float32) * scale
    fine_angle = (rows[:, None] * fine[None, :] % length).astype(jnp.float32) * scale
    c_hi, s_hi = (jnp.cos(coarse_angle)[:, :, None], jnp.sin(coarse_angle)[:, :, None])
    c_lo, s_lo = (jnp.cos(fine_angle)[:, None, :], jnp.sin(fine_angle)[:, None, :])
    shape = (rows.shape[0], col_count)
    cosine = (c_hi * c_lo - s_hi * s_lo).reshape(shape)
    sine = (s_hi * c_lo + c_hi * s_lo).reshape(shape)
    return (cosine, sine)


def forward_matrix(length):
    cosine, sine = phase_table(jnp.arange(length // 2, dtype=jnp.int32), length, length)
    return jnp.concatenate([cosine, -sine], axis=0).astype(jnp.bfloat16)


def inverse_matrix(length, first_lag, lag_count, seg_total):
    half_bins = length // 2
    lags = jnp.arange(lag_count, dtype=jnp.int32) + first_lag
    cosine, sine = phase_table(lags, half_bins, length)
    bin_index = jnp.arange(half_bins)[None, :]
    weights = jnp.where(bin_index == 0, 1.0, 2.0).astype(jnp.float32) * (
        1.0 / math.sqrt(half_bins * seg_total)
    )
    return jnp.concatenate([weights * cosine, -weights * sine], axis=1)


def whiten(spectra, band_width):
    half_bins = spectra.shape[-2] // 2
    real_rows = spectra[..., :half_bins, :]
    imaginary = spectra[..., half_bins:, :]
    energy = real_rows * real_rows + imaginary * imaginary
    grouped = energy.shape[:-2] + (half_bins // band_width, band_width, energy.shape[-1])
    band_power = jnp.mean(energy.reshape(grouped), axis=-2, keepdims=True)
    inverse_rms = jnp.broadcast_to(lax.rsqrt(band_power + power_floor), grouped).reshape(
        energy.shape
    )
    return (spectra * jnp.concatenate([inverse_rms, inverse_rms], axis=-2)).astype(jnp.bfloat16)


def cross_terms(first_part, second_part):
    half_bins = first_part.shape[-2] // 2
    first_real = first_part[..., :half_bins, :].astype(jnp.float32)
    first_imag = first_part[..., half_bins:, :].astype(jnp.float32)
    second_real = second_part[..., :half_bins, :].astype(jnp.float32)
    second_imag = second_part[..., half_bins:, :].astype(jnp.float32)
    real_sum = first_real * second_real + first_imag * second_imag
    imag_sum = first_imag * second_real - first_real * second_imag
    return jnp.concatenate([real_sum, imag_sum], axis=-2)


def bucket_select(owner_ids, owner_count, capacity):
    onehot = (owner_ids[:, None] == jnp.arange(owner_count, dtype=jnp.int32)[None, :]).astype(
        jnp.int32
    )
    slot_rank = jnp.sum((jnp.cumsum(onehot, axis=0, dtype=jnp.int32) - 1) * onehot, axis=1)
    slot_id = owner_ids * capacity + slot_rank
    return (
        slot_id[None, :] == jnp.arange(owner_count * capacity, dtype=jnp.int32)[:, None]
    ).astype(jnp.bfloat16)


def tile_ring(mesh):
    count = mesh.shape["tile"]
    try:
        column = mesh.devices.reshape(count, -1)[:, 0]
        spots = [tuple((int(c) for c in d.coords)) for d in column]
    except (AttributeError, TypeError):
        return list(range(count))
    near = [
        [j for j in range(count) if sum((abs(a - b) for a, b in zip(spots[i], spots[j]))) == 1]
        for i in range(count)
    ]
    path, seen, budget = ([0], {0}, [20000])

    def extend():
        budget[0] -= 1
        if budget[0] < 0:
            return False
        if len(path) == count:
            return count < 3 or 0 in near[path[-1]]
        options = [j for j in near[path[-1]] if j not in seen]
        options.sort(key=lambda j: sum((1 for k in near[j] if k not in seen)))
        for j in options:
            path.append(j)
            seen.add(j)
            if extend():
                return True
            path.pop()
            seen.discard(j)
        return False

    return path if extend() else list(range(count))


def make_per_device(ring):
    count = len(ring)
    block_of = [0] * count
    for place, device in enumerate(ring):
        block_of[device] = place
    to_prev = [(ring[r], ring[(r - 1) % count]) for r in range(count)]
    to_next = [(ring[r], ring[(r + 1) % count]) for r in range(count)]

    def per_device(records, pair_first, pair_offset, owners):
        tile_count = lax.axis_size("tile")
        win_count = lax.axis_size("win")
        length = records.shape[1] * tile_count
        seg_total = records.shape[0] * win_count
        block = records.shape[2] // tile_count
        half = block // 2
        my_block = jnp.asarray(block_of, dtype=jnp.int32)[lax.axis_index("tile")]
        shifted = jnp.roll(records, -half, axis=2).reshape(
            records.shape[0], records.shape[1], tile_count, block
        )
        outgoing = jnp.concatenate([shifted[:, :, b] for b in block_of], axis=2)
        forward = forward_matrix(length)
        spectra = jnp.einsum(
            "fn,snc->sfc",
            forward,
            lax.all_to_all(outgoing, "tile", split_axis=2, concat_axis=1, tiled=True),
            preferred_element_type=jnp.float32,
        )
        whitened = whiten(spectra, BAND)
        from_prev = lax.ppermute(whitened[:, :, half:], "tile", to_next)
        from_next = lax.ppermute(whitened[:, :, :half], "tile", to_prev)
        joined = jnp.concatenate([from_prev, whitened, from_next], axis=2)
        all_first = lax.all_gather(pair_first, "tile")
        all_offset = lax.all_gather(pair_offset, "tile")
        all_owners = lax.all_gather(owners[:, 0], "tile")
        my_first = lax.dynamic_index_in_dim(all_first, my_block, 0, keepdims=False)
        my_offset = lax.dynamic_index_in_dim(all_offset, my_block, 0, keepdims=False)
        my_owners = lax.dynamic_index_in_dim(all_owners, my_block, 0, keepdims=False)
        channel_ids = jnp.arange(joined.shape[2], dtype=jnp.int32)[:, None]
        pick_first = (channel_ids == my_first[None, :]).astype(jnp.bfloat16)
        pick_second = (channel_ids == (my_first + my_offset)[None, :]).astype(jnp.bfloat16)
        first_part = jnp.einsum(
            "sfc,cp->sfp", joined, pick_first, preferred_element_type=jnp.float32
        )
        second_part = jnp.einsum(
            "sfc,cp->sfp", joined, pick_second, preferred_element_type=jnp.float32
        )
        cross = jnp.sum(cross_terms(first_part, second_part), axis=0)
        lag_count = length // win_count
        stacked = lax.psum(cross, "win")
        inverse = inverse_matrix(length, lax.axis_index("win") * lag_count, lag_count, seg_total)
        correlation = jnp.dot(inverse, stacked, precision=lax.Precision.HIGHEST)
        capacity = 5 * pair_first.shape[0] // (2 * tile_count)
        chooser = bucket_select(my_owners, tile_count, capacity)
        picked = lax.dot_general(
            chooser,
            correlation.astype(jnp.bfloat16),
            (((1,), (1,)), ((), ())),
            preferred_element_type=jnp.float32,
        )
        buckets = picked.astype(jnp.bfloat16).reshape(tile_count, capacity, lag_count)
        received = lax.all_to_all(buckets, "tile", split_axis=0, concat_axis=0, tiled=True)
        ordered = jnp.stack([received[d] for d in ring], axis=0)
        return ordered[None]

    return per_device


def solution(mesh):
    placed = (P("win", "tile", None), P("tile"), P("tile"), P("tile", None))
    return jax.shard_map(
        make_per_device(tile_ring(mesh)),
        mesh=mesh,
        in_specs=placed,
        out_specs=P("tile", None, None, "win"),
        check_vma=False,
    )
```

profile of v0, /device:TPU:0, one launch (start us, length us, event | category | flops | bytes accessed | tf_op | source)
XLA Modules:
  0.0 392.1 jit_solution(10754620685707993327)
XLA Ops:
  6.5 4.3 %slice.87 = bf16[4,256,1920]{2,1,0:T(8,128)(2,1)} slice(bf16[4,256,2048]{2,1,0:T(8,128)(2,1)} %param.5), slice={[0:4], [0:256], [128:2048]} | slice | bytes 7864320 | tf_op jit(solution)/shard_map/jit(_roll_static)/slice | solution.py:126
  10.8 6.3 %copy.65 = bf16[4,256,1920]{1,2,0:T(8,128)(2,1)} copy(bf16[4,256,1920]{2,1,0:T(8,128)(2,1)} %slice.87) | data formatting | bytes 7864320
  17.1 0.1 copy.66
  17.3 2.4 pad_maximum_fusion.1
  20.0 17.2 %copy.52 = bf16[4,256,2048]{1,0,2:T(4,128)(2,1)} copy(bf16[4,256,2048]{1,2,0:T(8,128)(2,1)S(1)} %fusion.15) | data formatting | bytes 8388608 | tf_op jit(solution)/shard_map/concatenate | solution.py:129
  37.2 7.3 %all-to-all-start = ((bf16[4,256,2048]{1,0,2:T(4,128)(2,1)}), bf16[4,256,2048]{1,0,2:T(4,128)(2,1)}, u32[]{:S(2)}, u32[]{:S(2)}) async-start(bf16[4,256,2048]{1,0,2:T(4,128)(2,1)} %copy.52), calls=%async_computation | async-start | bytes 8388608 | tf_op jit(solution)/shard_map/all_to_all | solution.py:134
  44.5 1.0 fusion.42
  45.6 0.6 fusion.51
  46.2 5.2 %subtract_convert_fusion = (bf16[1024,32,64]{0,2,1:T(8,128)(2,1)}, bf16[1024,32,64]{0,2,1:T(8,128)(2,1)}) fusion(f32[1024,64]{0,1:T(8,128)S(1)} %get-tuple-element.21, f32[1024,32]{0,1:T(8,128)S(1)} %get-tuple-element.20, f32[1024,64]{0,1:T(8,128)S(1)} %get-tuple-element.22, f32[1024,32]{0,1:T(8,128)S(1)} %get-tuple-element.19), kind=kLoop, calls=%fused_computation.9 | loop fusion | flops 18874368 | bytes 9175040 | tf_op jit(solution)/shard_map/convert.3
  51.4 6.5 %copy.55 = bf16[1024,2048]{1,0:T(8,128)(2,1)} copy(bf16[1024,2048]{0,1:T(8,128)(2,1)} %bitcast.102) | data formatting | bytes 8388608 | tf_op jit(solution)/shard_map/sub | solution.py:21
  57.8 6.5 %copy.56 = bf16[1024,2048]{1,0:T(8,128)(2,1)} copy(bf16[1024,2048]{0,1:T(8,128)(2,1)} %bitcast.101) | data formatting | bytes 8388608 | tf_op jit(solution)/shard_map/neg | solution.py:28
  64.3 73.5 %all-to-all-done = bf16[4,256,2048]{1,0,2:T(4,128)(2,1)} async-done(((bf16[4,256,2048]{1,0,2:T(4,128)(2,1)}), bf16[4,256,2048]{1,0,2:T(4,128)(2,1)}, u32[]{:S(2)}, u32[]{:S(2)}) %all-to-all-start) | async-done | bytes 4194336 | tf_op jit(solution)/shard_map/all_to_all | solution.py:134
  137.8 2.7 copy.53
  140.5 2.7 copy.73
  143.2 1.0 copy-done.3
  144.2 11.7 %fusion.4 = f32[4,2048,256]{1,2,0:T(8,128)S(1)} fusion(bf16[4,2048,256]{1,2,0:T(8,128)(2,1)} %bitcast.105, bf16[1024,2048]{1,0:T(8,128)(2,1)} %copy.56, bf16[1024,2048]{1,0:T(8,128)(2,1)S(1)} %copy-done.3), kind=kOutput, calls=%fused_computation.10 | convolution fusion | flops 8606711808 | bytes 20971520 | tf_op jit(solution)/shard_map/fn,snc->sfc/dot_general | solution.py:131
  156.0 3.2 copy-done
  159.2 2.9 fusion.5
  162.1 5.4 %copy.57 = f32[4,1024,256]{2,1,0:T(8,128)} copy(f32[4,1024,256]{1,2,0:T(8,128)} %fusion.5) | data formatting | bytes 8388608 | tf_op jit(solution)/shard_map/add | solution.py:46
  167.5 2.7 bitcast_reduce_fusion
  170.2 2.3 broadcast_in_dim.12
  172.5 5.4 %copy.58 = f32[4,1024,256]{1,2,0:T(8,128)} copy(f32[4,1024,256]{2,1,0:T(8,128)} %bitcast.104) | data formatting | bytes 8388608 | tf_op jit(solution)/shard_map/reshape | solution.py:49
  177.9 7.0 %fusion.3 = bf16[4,2048,256]{1,2,0:T(8,128)(2,1)S(1)} fusion(f32[4,2048,256]{1,2,0:T(8,128)} %copy-done, f32[4,1024,256]{1,2,0:T(8,128)} %copy.58), kind=kLoop, calls=%fused_computation.5 | loop fusion | flops 6291456 | bytes 16777216 | tf_op jit(solution)/shard_map/convert_element_type | solution.py:52
  184.9 2.1 fusion.66
  187.0 0.5 copy-done.1
  187.5 1.5 collective-permute-start
  189.0 0.6 collective-permute-start.1
  189.5 0.6 dynamic_slice.13
  191.4 56.6 %all-gather = s32[2048,1]{0,1:T(1,128)S(1)} all-gather(s32[256,1]{0,1:T(1,128)S(1)} %copy-done.5), channel_id=2, replica_groups=mesh['tile'=8,'win'=4] {'tile'}, dimensions={0}, use_global_device_ids=true | all-gather | bytes 9216 | tf_op jit(solution)/shard_map/all_gather | solution.py:143
  248.0 0.6 broadcast.396
  248.6 0.7 reduce.5
  250.0 0.6 reduce-window.6
  250.6 0.2 slice_reduce_fusion
  250.9 16.8 %all-gather.3 = s32[8,1,256]{2,1,0:T(1,128)S(1)} all-gather(s32[1,1,256]{2,1,0:T(1,128)S(1)} %bitcast.111), channel_id=3, replica_groups=mesh['tile'=8,'win'=4] {'tile'}, dimensions={0}, use_global_device_ids=true | all-gather | bytes 9216 | tf_op jit(solution)/shard_map/all_gather | solution.py:141
  267.7 18.0 %all-gather.4 = s32[8,1,256]{2,1,0:T(1,128)S(1)} all-gather(s32[1,1,256]{2,1,0:T(1,128)S(1)} %bitcast.112), channel_id=4, replica_groups=mesh['tile'=8,'win'=4] {'tile'}, dimensions={0}, use_global_device_ids=true | all-gather | bytes 9216 | tf_op jit(solution)/shard_map/all_gather | solution.py:142
  285.8 0.2 fusion.58
  286.0 5.1 %fusion.11 = f32[4,2048,256]{2,1,0:T(8,128)S(1)} fusion(bf16[4,2048,128]{1,2,0:T(8,128)(2,1)} %collective-permute-done.1, bf16[4,2048,256]{1,2,0:T(8,128)(2,1)} %copy-done.1, bf16[4,2048,128]{1,2,0:T(8,128)(2,1)} %collective-permute-done, s32[256]{0:T(256)S(1)} %bitcast.114), kind=kOutput, calls=%fused_computation.23 | convolution fusion | flops 2172780544 | bytes 16778240 | tf_op jit(solution)/shard_map/sfc,cp->sfp/dot_general | solution.py:150
  291.2 6.2 %fusion.10 = f32[4,2048,256]{2,1,0:T(8,128)} fusion(bf16[4,2048,128]{1,2,0:T(8,128)(2,1)} %collective-permute-done.1, bf16[4,2048,256]{1,2,0:T(8,128)(2,1)S(1)} %copy-done.2, bf16[4,2048,128]{1,2,0:T(8,128)(2,1)} %collective-permute-done, s32[256]{0:T(256)S(1)} %bitcast.113), kind=kOutput, calls=%fused_computation.22 | convolution fusion | flops 2172780544 | bytes 16778240 | tf_op jit(solution)/shard_map/sfc,cp->sfp/dot_general | solution.py:153
  297.4 4.0 %multiply_add_fusion = (f32[4,1024,256]{2,1,0:T(8,128)S(1)}, f32[4,1024,256]{2,1,0:T(8,128)S(1)}) fusion(f32[4,2048,256]{2,1,0:T(8,128)} %fusion.10, f32[4,2048,256]{2,1,0:T(8,128)S(1)} %fusion.11), kind=kLoop, calls=%fused_computation.21 | loop fusion | flops 6291456 | bytes 25165824 | tf_op jit(solution)/shard_map/add | solution.py:61
  301.4 2.0 maximum_reduce_fusion
  303.4 0.5 fusion.53
  304.0 0.6 multiply_subtract_fusion.1
  304.6 1.6 bitcast_multiply_fusion
  306.2 46.0 %all-reduce.2.cloned.1.call-done = f32[2048,256]{1,0:T(8,128)} async-done(((f32[2048,256]{1,0:T(8,128)}), f32[2048,256]{1,0:T(8,128)}) %all-reduce.2.cloned.1.call-update) | async-done | bytes 2097168 | tf_op jit(solution)/shard_map/psum | solution.py:158
  352.2 8.9 %fusion.12 = bf16[512,256]{1,0:T(8,128)(2,1)S(1)} fusion(f32[2048,256]{1,0:T(8,128)} %all-reduce.2.cloned.1.call-done, f32[512,1024]{0,1:T(8,128)S(1)} %get-tuple-element.23, f32[512,1024]{0,1:T(8,128)} %get-tuple-element.24), kind=kOutput, calls=%fused_computation.29 | convolution fusion | flops 3222405120 | bytes 6553600 | tf_op jit(solution)/shard_map/dot_general | solution.py:160
  361.1 0.4 convolution_convert_fusion
  361.5 22.8 %all_to_all.23 = bf16[8,80,512]{2,1,0:T(8,128)(2,1)S(1)} all-to-all(bf16[8,80,512]{2,1,0:T(8,128)(2,1)S(1)} %bitcast.106), channel_id=1, replica_groups=mesh['tile'=8,'win'=4] {'tile'}, dimensions={0} | all-to-all | bytes 1310720 | tf_op jit(solution)/shard_map/all_to_all | solution.py:170
  384.4 0.8 copy-done.4
  (49 shorter events, 0.7 us)
Async XLA Ops:
  10.8 6.3 %slice-start = ((bf16[4,256,2048]{2,1,0:T(8,128)(2,1)}), bf16[4,256,128]{2,1,0:T(8,128)(2,1)S(1)}, s32[]{:S(2)}) async-start(bf16[4,256,2048]{2,1,0:T(8,128)(2,1)} %param.5), calls=%async_computation.3 | async-start | bytes 524288 | tf_op jit(solution)/shard_map/jit(_roll_static)/slice | solution.py:126
  37.2 100.6 %all-to-all-start = ((bf16[4,256,2048]{1,0,2:T(4,128)(2,1)}), bf16[4,256,2048]{1,0,2:T(4,128)(2,1)}, u32[]{:S(2)}, u32[]{:S(2)}) async-start(bf16[4,256,2048]{1,0,2:T(4,128)(2,1)} %copy.52), calls=%async_computation | async-start | bytes 8388608 | tf_op jit(solution)/shard_map/all_to_all | solution.py:134
  44.5 307.7 %all-reduce.2.cloned.1.call-start = ((), (), s32[]{:S(2)}) async-start(), calls=%async_computation.2 | async-start | bytes 4194304 | tf_op jit(solution)/shard_map/psum | solution.py:158
  140.5 3.7 copy-start.3
  156.0 3.2 copy-start
  184.9 2.6 copy-start.1
  184.9 4.7 %copy-start.8 = (s32[8]{0:T(128)S(1)}, s32[8]{0:T(128)}, u32[]{:S(2)}) copy-start(s32[8]{0:T(128)} %constant.94.clone) | copy-start | bytes 100
  184.9 6.5 %copy-start.5 = (s32[256,1]{0,1:T(1,128)S(1)}, s32[256,1]{0,1:T(1,128)}, u32[]{:S(2)}) copy-start(s32[256,1]{0,1:T(1,128)} %param.8) | copy-start | bytes 3076
  184.9 66.0 %copy-start.6 = (s32[256]{0:T(256)S(1)}, s32[256]{0:T(256)}, u32[]{:S(2)}) copy-start(s32[256]{0:T(256)} %param.6) | copy-start | bytes 3076
  184.9 82.8 %copy-start.7 = (s32[256]{0:T(256)S(1)}, s32[256]{0:T(256)}, u32[]{:S(2)}) copy-start(s32[256]{0:T(256)} %param.7) | copy-start | bytes 3076
  187.5 98.5 %collective-permute-start = (bf16[4,2048,128]{1,2,0:T(8,128)(2,1)}, bf16[4,2048,128]{1,2,0:T(8,128)(2,1)}, u32[]{:S(2)}, u32[]{:S(2)}) collective-permute-start(bf16[4,2048,128]{1,2,0:T(8,128)(2,1)} %get-tuple-element.7), channel_id=1, source_target_pairs={{0,4},{4,12},{12,20},{20,28},{28,24},{24,16},{16,8},{8,0},{1,5},{5... | collective-permute-start | bytes 6291464 | tf_op jit(solution)/shard_map/ppermute | solution.py:138
  189.0 97.1 %collective-permute-start.1 = (bf16[4,2048,128]{1,2,0:T(8,128)(2,1)S(1)}, bf16[4,2048,128]{1,2,0:T(8,128)(2,1)}, u32[]{:S(2)}, u32[]{:S(2)}) collective-permute-start(bf16[4,2048,128]{1,2,0:T(8,128)(2,1)S(1)} %get-tuple-element.8), channel_id=1, source_target_pairs={{0,8},{4,0},{12,4},{20,12},{28,20},{24,28},{16,24},{8,16},{1,9},{5... | collective-permute-start | bytes 6291464 | tf_op jit(solution)/shard_map/ppermute | solution.py:139
  286.0 5.1 %copy-start.2 = (bf16[4,2048,256]{1,2,0:T(8,128)(2,1)S(1)}, bf16[4,2048,256]{1,2,0:T(8,128)(2,1)}, u32[]{:S(2)}) copy-start(bf16[4,2048,256]{1,2,0:T(8,128)(2,1)} %copy-done.1) | copy-start | bytes 12582916
  384.4 0.8 copy-start.4
Sparse Core Ops, SparseCore 0:
  303.6 48.6 all-reduce.1
where the time goes:
time: 393 us; the launch traced here: 392 us
  waiting for transfers between devices  119 us (30%)
  blocking collectives  114 us (29%)
  local copies, waits for them, and re-layouts  68.7 us (17%)
  other arithmetic  32.3 us (8%)
  matrix products  32.3 us (8%)
  between operations  15.7 us (4%)
  starting transfers between devices  9.37 us (2%)
    all_to_all x1, waiting for transfers between devices, per_device(): lax.all_to_all(outgoing, 'tile', split_axis=2, concat_axis=1, tiled=True)  73.5 us
    all_gather x1, blocking collectives, per_device(): all_owners = lax.all_gather(owners[:, 0], 'tile')  56.6 us
    psum x1, waiting for transfers between devices, per_device(): stacked = lax.psum(cross, 'win')  46 us
    all_to_all x1, blocking collectives, per_device(): lax.all_to_all(buckets, 'tile', split_axis=0, concat_axis=0, tiled=True)  22.8 us
    all_gather x1, blocking collectives, per_device(): all_offset = lax.all_gather(pair_offset, 'tile')  18 us
    concatenate x2, local copies, waits for them, and re-layouts, per_device(): outgoing = jnp.concatenate([shifted[:, :, b] for b in block_of], axis=2)  17.2 us
    all_gather x1, blocking collectives, per_device(): all_first = lax.all_gather(pair_first, 'tile')  16.8 us
    unnamed x33, local copies, waits for them, and re-layouts  12.3 us
  transfers between devices with their start and end apart: 4, of which 2 were waited for; matrix products, arithmetic and copies ran while one was open for 7% of the time, Pallas kernels for 0%

commit v1 on v0

--- a/solution.py
+++ b/solution.py
@@ -155,7 +155,9 @@
         )
         cross = jnp.sum(cross_terms(first_part, second_part), axis=0)
         lag_count = length // win_count
-        stacked = lax.psum(cross, "win")
+        stacked = cross
+        for hop in (1, 2):
+            stacked = stacked + lax.ppermute(stacked, "win", [(dev, dev ^ hop) for dev in range(4)])
         inverse = inverse_matrix(length, lax.axis_index("win") * lag_count, lag_count, seg_total)
         correlation = jnp.dot(inverse, stacked, precision=lax.Precision.HIGHEST)
         capacity = 5 * pair_first.shape[0] // (2 * tile_count)

time: 393 us -> 369 us (0.939)
  between operations: 15.7 us -> 2.35 us
  blocking collectives: 114 us -> 107 us
  waiting for transfers between devices: 119 us -> 115 us
    psum x1 -> x0, waiting for transfers between devices: 46 us -> none  [per_device(): stacked = lax.psum(cross, 'win')]
    ppermute x0 -> x2, waiting for transfers between devices: none -> 40.9 us  [per_device(): lax.ppermute(stacked, 'win', [(dev, dev ^ hop) for dev in range(4)])]
    all_gather x1, blocking collectives: 16.8 us -> 55.9 us  [per_device(): all_first = lax.all_gather(pair_first, 'tile')]
    all_gather x1, blocking collectives: 56.6 us -> 17.8 us  [per_device(): all_owners = lax.all_gather(owners[:, 0], 'tile')]
    all_to_all x1, blocking collectives: 22.8 us -> 16.5 us  [per_device(): lax.all_to_all(buckets, 'tile', split_axis=0, concat_axis=0, tiled=True)]
  transfers between devices with their start and end apart: 4 -> 5, of which waited for: 2 -> 2; matrix products, arithmetic and copies ran while one was open for 7% -> 7% of each run, Pallas kernels for 0% -> 0%
where the time goes in v1:
time: 369 us; the launch traced here: 368 us
  waiting for transfers between devices  115 us (31%)
  blocking collectives  107 us (29%)
  local copies, waits for them, and re-layouts  68.7 us (19%)
  other arithmetic  32.7 us (9%)
  matrix products  31.8 us (9%)
  starting transfers between devices  10.9 us (3%)
    all_to_all x1, waiting for transfers between devices, per_device(): lax.all_to_all(outgoing, 'tile', split_axis=2, concat_axis=1, tiled=True)  73.7 us
    all_gather x1, blocking collectives, per_device(): all_first = lax.all_gather(pair_first, 'tile')  55.9 us
    ppermute x2, waiting for transfers between devices, per_device(): lax.ppermute(stacked, 'win', [(dev, dev ^ hop) for dev in range(4)])  40.9 us
    all_gather x1, blocking collectives, per_device(): all_owners = lax.all_gather(owners[:, 0], 'tile')  17.8 us
    concatenate x2, local copies, waits for them, and re-layouts, per_device(): outgoing = jnp.concatenate([shifted[:, :, b] for b in block_of], axis=2)  17.2 us
    all_gather x1, blocking collectives, per_device(): all_offset = lax.all_gather(pair_offset, 'tile')  16.8 us
    all_to_all x1, blocking collectives, per_device(): lax.all_to_all(buckets, 'tile', split_axis=0, concat_axis=0, tiled=True)  16.5 us
    unnamed x33, local copies, waits for them, and re-layouts  12.3 us
  transfers between devices with their start and end apart: 5, of which 2 were waited for; matrix products, arithmetic and copies ran while one was open for 7% of the time, Pallas kernels for 0%

profile of v1, /device:TPU:0, one launch (start us, length us, event | category | flops | bytes accessed | tf_op | source)
XLA Modules:
  0.0 368.0 jit_solution(16272401458797594602)
XLA Ops:
  0.0 4.3 %slice.87 = bf16[4,256,1920]{2,1,0:T(8,128)(2,1)} slice(bf16[4,256,2048]{2,1,0:T(8,128)(2,1)} %param.5), slice={[0:4], [0:256], [128:2048]} | slice | bytes 7864320 | tf_op jit(solution)/shard_map/jit(_roll_static)/slice | solution.py:126
  4.3 6.3 %copy.65 = bf16[4,256,1920]{1,2,0:T(8,128)(2,1)} copy(bf16[4,256,1920]{2,1,0:T(8,128)(2,1)} %slice.87) | data formatting | bytes 7864320
  10.8 2.4 pad_maximum_fusion.1
  13.5 17.2 %copy.52 = bf16[4,256,2048]{1,0,2:T(4,128)(2,1)} copy(bf16[4,256,2048]{1,2,0:T(8,128)(2,1)S(1)} %fusion.18) | data formatting | bytes 8388608 | tf_op jit(solution)/shard_map/concatenate | solution.py:129
  30.7 7.3 %all-to-all-start = ((bf16[4,256,2048]{1,0,2:T(4,128)(2,1)}), bf16[4,256,2048]{1,0,2:T(4,128)(2,1)}, u32[]{:S(2)}, u32[]{:S(2)}) async-start(bf16[4,256,2048]{1,0,2:T(4,128)(2,1)} %copy.52), calls=%async_computation | async-start | bytes 8388608 | tf_op jit(solution)/shard_map/all_to_all | solution.py:134
  38.0 1.0 fusion.45
  39.0 0.6 fusion.54
  39.6 5.0 %subtract_convert_fusion = (bf16[1024,32,64]{0,2,1:T(8,128)(2,1)}, bf16[1024,32,64]{0,2,1:T(8,128)(2,1)}) fusion(f32[1024,64]{0,1:T(8,128)S(1)} %get-tuple-element.21, f32[1024,32]{0,1:T(8,128)S(1)} %get-tuple-element.20, f32[1024,64]{0,1:T(8,128)S(1)} %get-tuple-element.22, f32[1024,32]{0,1:T(8,128)S(1)} %get-tuple-element.19), kind=kLoop, calls=%fused_computation.9 | loop fusion | flops 18874368 | bytes 9175040 | tf_op jit(solution)/shard_map/convert.3
  44.6 6.5 %copy.55 = bf16[1024,2048]{1,0:T(8,128)(2,1)} copy(bf16[1024,2048]{0,1:T(8,128)(2,1)} %bitcast.101) | data formatting | bytes 8388608 | tf_op jit(solution)/shard_map/sub | solution.py:21
  51.1 6.5 %copy.56 = bf16[1024,2048]{1,0:T(8,128)(2,1)} copy(bf16[1024,2048]{0,1:T(8,128)(2,1)} %bitcast.100) | data formatting | bytes 8388608 | tf_op jit(solution)/shard_map/neg | solution.py:28
  57.6 73.7 %all-to-all-done = bf16[4,256,2048]{1,0,2:T(4,128)(2,1)} async-done(((bf16[4,256,2048]{1,0,2:T(4,128)(2,1)}), bf16[4,256,2048]{1,0,2:T(4,128)(2,1)}, u32[]{:S(2)}, u32[]{:S(2)}) %all-to-all-start) | async-done | bytes 4194336 | tf_op jit(solution)/shard_map/all_to_all | solution.py:134
  131.3 2.7 copy.53
  134.0 2.7 copy.73
  136.7 1.0 copy-done.3
  137.7 11.8 %fusion.4 = f32[4,2048,256]{1,2,0:T(8,128)S(1)} fusion(bf16[4,2048,256]{1,2,0:T(8,128)(2,1)} %bitcast.104, bf16[1024,2048]{1,0:T(8,128)(2,1)} %copy.56, bf16[1024,2048]{1,0:T(8,128)(2,1)S(1)} %copy-done.3), kind=kOutput, calls=%fused_computation.10 | convolution fusion | flops 8606711808 | bytes 20971520 | tf_op jit(solution)/shard_map/fn,snc->sfc/dot_general | solution.py:131
  149.5 3.2 copy-done
  152.7 2.9 fusion.5
  155.6 5.4 %copy.57 = f32[4,1024,256]{2,1,0:T(8,128)} copy(f32[4,1024,256]{1,2,0:T(8,128)} %fusion.5) | data formatting | bytes 8388608 | tf_op jit(solution)/shard_map/add | solution.py:46
  161.0 2.7 bitcast_reduce_fusion
  163.8 2.3 broadcast_in_dim.12
  166.1 5.4 %copy.58 = f32[4,1024,256]{1,2,0:T(8,128)} copy(f32[4,1024,256]{2,1,0:T(8,128)} %bitcast.103) | data formatting | bytes 8388608 | tf_op jit(solution)/shard_map/reshape | solution.py:49
  171.5 7.0 %fusion.3 = bf16[4,2048,256]{1,2,0:T(8,128)(2,1)S(1)} fusion(f32[4,2048,256]{1,2,0:T(8,128)} %copy-done, f32[4,1024,256]{1,2,0:T(8,128)} %copy.58), kind=kLoop, calls=%fused_computation.5 | loop fusion | flops 6291456 | bytes 16777216 | tf_op jit(solution)/shard_map/convert_element_type | solution.py:52
  178.6 2.1 fusion.69
  180.6 0.5 copy-done.1
  181.1 1.5 collective-permute-start
  182.6 0.6 collective-permute-start.1
  183.2 0.6 dynamic_slice.13
  185.7 55.9 %all-gather.3 = s32[8,1,256]{2,1,0:T(1,128)S(1)} all-gather(s32[1,1,256]{2,1,0:T(1,128)S(1)} %bitcast.110), channel_id=3, replica_groups=mesh['tile'=8,'win'=4] {'tile'}, dimensions={0}, use_global_device_ids=true | all-gather | bytes 9216 | tf_op jit(solution)/shard_map/all_gather | solution.py:141
  241.7 16.8 %all-gather.4 = s32[8,1,256]{2,1,0:T(1,128)S(1)} all-gather(s32[1,1,256]{2,1,0:T(1,128)S(1)} %bitcast.111), channel_id=4, replica_groups=mesh['tile'=8,'win'=4] {'tile'}, dimensions={0}, use_global_device_ids=true | all-gather | bytes 9216 | tf_op jit(solution)/shard_map/all_gather | solution.py:142
  258.5 5.1 %fusion.11 = f32[4,2048,256]{2,1,0:T(8,128)S(1)} fusion(bf16[4,2048,128]{1,2,0:T(8,128)(2,1)} %collective-permute-done.1, bf16[4,2048,256]{1,2,0:T(8,128)(2,1)} %copy-done.1, bf16[4,2048,128]{1,2,0:T(8,128)(2,1)} %collective-permute-done, s32[256]{0:T(256)S(1)} %bitcast.113), kind=kOutput, calls=%fused_computation.23 | convolution fusion | flops 2172780544 | bytes 16778240 | tf_op jit(solution)/shard_map/sfc,cp->sfp/dot_general | solution.py:150
  263.6 6.3 %fusion.10 = f32[4,2048,256]{2,1,0:T(8,128)} fusion(bf16[4,2048,128]{1,2,0:T(8,128)(2,1)} %collective-permute-done.1, bf16[4,2048,256]{1,2,0:T(8,128)(2,1)S(1)} %copy-done.2, bf16[4,2048,128]{1,2,0:T(8,128)(2,1)} %collective-permute-done, s32[256]{0:T(256)S(1)} %bitcast.112), kind=kOutput, calls=%fused_computation.22 | convolution fusion | flops 2172780544 | bytes 16778240 | tf_op jit(solution)/shard_map/sfc,cp->sfp/dot_general | solution.py:153
  269.9 4.0 %multiply_add_fusion = (f32[4,1024,256]{2,1,0:T(8,128)S(1)}, f32[4,1024,256]{2,1,0:T(8,128)S(1)}) fusion(f32[4,2048,256]{2,1,0:T(8,128)} %fusion.10, f32[4,2048,256]{2,1,0:T(8,128)S(1)} %fusion.11), kind=kLoop, calls=%fused_computation.21 | loop fusion | flops 6291456 | bytes 25165824 | tf_op jit(solution)/shard_map/add | solution.py:61
  273.9 0.7 maximum_reduce_fusion
  274.7 17.8 %all-gather = s32[2048,1]{0,1:T(1,128)S(1)} all-gather(s32[256,1]{0,1:T(1,128)S(1)} %copy-done.7), channel_id=2, replica_groups=mesh['tile'=8,'win'=4] {'tile'}, dimensions={0}, use_global_device_ids=true | all-gather | bytes 9216 | tf_op jit(solution)/shard_map/all_gather | solution.py:143
  292.5 0.5 broadcast.396
  293.0 0.7 reduce.5
  293.7 0.6 reduce-window.6
  294.3 3.2 add.138
  297.4 1.5 collective-permute-start.3
  299.3 0.2 fusion.61
  299.6 0.5 fusion.56
  300.1 0.6 multiply_subtract_fusion.1
  300.7 0.3 bitcast_multiply_fusion
  301.0 40.9 %collective-permute-done.3 = f32[2048,256]{1,0:T(8,128)S(1)} collective-permute-done((f32[2048,256]{1,0:T(8,128)}, f32[2048,256]{1,0:T(8,128)S(1)}, u32[]{:S(2)}, u32[]{:S(2)}) %collective-permute-start.3) | collective-permute-done | bytes 2097184 | tf_op jit(solution)/shard_map/ppermute | solution.py:160
  341.9 8.3 %fusion.13 = bf16[512,256]{1,0:T(8,128)(2,1)S(1)} fusion(f32[2048,256]{1,0:T(8,128)} %add.138, f32[2048,256]{1,0:T(8,128)S(1)} %collective-permute-done.3, f32[512,1024]{0,1:T(8,128)S(1)} %get-tuple-element.23, f32[512,1024]{0,1:T(8,128)S(1)} %get-tuple-element.24), kind=kOutput, calls=%fused_computation.30 | convolution fusion | flops 3222929408 | bytes 8650752 | tf_op jit(solution)/shard_map/dot_general | solution.py:162
  350.2 0.4 convolution_convert_fusion
  350.6 16.5 %all_to_all.23 = bf16[8,80,512]{2,1,0:T(8,128)(2,1)S(1)} all-to-all(bf16[8,80,512]{2,1,0:T(8,128)(2,1)S(1)} %bitcast.105), channel_id=1, replica_groups=mesh['tile'=8,'win'=4] {'tile'}, dimensions={0} | all-to-all | bytes 1310720 | tf_op jit(solution)/shard_map/all_to_all | solution.py:172
  367.2 0.8 copy-done.4
  (51 shorter events, 1.0 us)
Async XLA Ops:
  4.3 6.3 %slice-start = ((bf16[4,256,2048]{2,1,0:T(8,128)(2,1)}), bf16[4,256,128]{2,1,0:T(8,128)(2,1)S(1)}, s32[]{:S(2)}) async-start(bf16[4,256,2048]{2,1,0:T(8,128)(2,1)} %param.5), calls=%async_computation.2 | async-start | bytes 524288 | tf_op jit(solution)/shard_map/jit(_roll_static)/slice | solution.py:126
  30.7 100.6 %all-to-all-start = ((bf16[4,256,2048]{1,0,2:T(4,128)(2,1)}), bf16[4,256,2048]{1,0,2:T(4,128)(2,1)}, u32[]{:S(2)}, u32[]{:S(2)}) async-start(bf16[4,256,2048]{1,0,2:T(4,128)(2,1)} %copy.52), calls=%async_computation | async-start | bytes 8388608 | tf_op jit(solution)/shard_map/all_to_all | solution.py:134
  134.0 3.7 %copy-start.3 = (bf16[1024,2048]{1,0:T(8,128)(2,1)S(1)}, bf16[1024,2048]{1,0:T(8,128)(2,1)}, u32[]{:S(2)}) copy-start(bf16[1024,2048]{1,0:T(8,128)(2,1)} %copy.55) | copy-start | bytes 12582916
  149.5 3.2 copy-start
  178.5 2.6 copy-start.1
  178.5 4.7 %copy-start.8 = (s32[8]{0:T(128)S(1)}, s32[8]{0:T(128)}, u32[]{:S(2)}) copy-start(s32[8]{0:T(128)} %constant.94.clone) | copy-start | bytes 100
  178.5 7.2 %copy-start.5 = (s32[256]{0:T(256)S(1)}, s32[256]{0:T(256)}, u32[]{:S(2)}) copy-start(s32[256]{0:T(256)} %param.6) | copy-start | bytes 3076
  178.5 63.1 %copy-start.6 = (s32[256]{0:T(256)S(1)}, s32[256]{0:T(256)}, u32[]{:S(2)}) copy-start(s32[256]{0:T(256)} %param.7) | copy-start | bytes 3076
  181.1 77.3 %collective-permute-start = (bf16[4,2048,128]{1,2,0:T(8,128)(2,1)}, bf16[4,2048,128]{1,2,0:T(8,128)(2,1)}, u32[]{:S(2)}, u32[]{:S(2)}) collective-permute-start(bf16[4,2048,128]{1,2,0:T(8,128)(2,1)} %get-tuple-element.7), channel_id=1, source_target_pairs={{0,4},{4,12},{12,20},{20,28},{28,24},{24,16},{16,8},{8,0},{1,5},{5... | collective-permute-start | bytes 6291464 | tf_op jit(solution)/shard_map/ppermute | solution.py:138
  182.6 75.9 %collective-permute-start.1 = (bf16[4,2048,128]{1,2,0:T(8,128)(2,1)S(1)}, bf16[4,2048,128]{1,2,0:T(8,128)(2,1)}, u32[]{:S(2)}, u32[]{:S(2)}) collective-permute-start(bf16[4,2048,128]{1,2,0:T(8,128)(2,1)S(1)} %get-tuple-element.8), channel_id=1, source_target_pairs={{0,8},{4,0},{12,4},{20,12},{28,20},{24,28},{16,24},{8,16},{1,9},{5... | collective-permute-start | bytes 6291464 | tf_op jit(solution)/shard_map/ppermute | solution.py:139
  258.5 5.1 %copy-start.2 = (bf16[4,2048,256]{1,2,0:T(8,128)(2,1)S(1)}, bf16[4,2048,256]{1,2,0:T(8,128)(2,1)}, u32[]{:S(2)}) copy-start(bf16[4,2048,256]{1,2,0:T(8,128)(2,1)} %copy-done.1) | copy-start | bytes 12582916
  273.9 0.8 copy-start.7
  274.6 19.7 %collective-permute-start.2 = (f32[2048,256]{1,0:T(8,128)S(1)}, f32[2048,256]{1,0:T(8,128)}, u32[]{:S(2)}, u32[]{:S(2)}) collective-permute-start(f32[2048,256]{1,0:T(8,128)S(1)} %maximum_reduce_fusion), channel_id=1, source_target_pairs={{0,1},{1,0},{2,3},{3,2},{4,5},{5,4},{6,7},{7,6},{8,9},{9,8},{10,11... | collective-permute-start | bytes 6291464 | tf_op jit(solution)/shard_map/ppermute | solution.py:160
  297.4 44.5 %collective-permute-start.3 = (f32[2048,256]{1,0:T(8,128)}, f32[2048,256]{1,0:T(8,128)S(1)}, u32[]{:S(2)}, u32[]{:S(2)}) collective-permute-start(f32[2048,256]{1,0:T(8,128)} %add.138), channel_id=1, source_target_pairs={{0,2},{1,3},{2,0},{3,1},{4,6},{5,7},{6,4},{7,5},{8,10},{9,11},{10,... | collective-permute-start | bytes 6291464 | tf_op jit(solution)/shard_map/ppermute | solution.py:160
  367.1 0.8 copy-start.4
